TPU v7x, 512 devices: a whole 4x4x16 slice. The times are simulated.
512 devices in a mesh: row: 32 (over y, x, core), col: 16 (over z).
Axes of the slice: x: 4, y: 4, z: 16, core: 2. Of those that a mesh axis runs over, the one named last changes fastest.
Arguments:
- queries: bfloat16 [512, 16, 1024], P('row', None, 'col'), may hold values from -30 to 30
- new_keys: bfloat16 [512, 1024], P('row', 'col'), may hold values from -6 to 6
- new_values: bfloat16 [512, 1024], P('row', 'col'), may hold values from -12 to 12
- cache_keys: bfloat16 [512, 128, 1024], P('row', None, 'col'), may hold values from -8 to 8
- cache_values: bfloat16 [512, 128, 1024], P('row', None, 'col'), may hold values from -12 to 12
- lengths: int32 [512], P('row'), may hold values from 64 to 128
- parents: int32 [512], P('row'), may hold values from 0 to 511, as said below
- residual: bfloat16 [512, 16, 1024], P('row', None, 'col'), may hold values from -20 to 20
- norm_gain: bfloat16 [16, 1024], P(None, 'col'), may hold values from 0.5 to 1.5
- vocab_weight: bfloat16 [16, 1024, 64128], P(None, 'col', 'row')
Outputs:
- logprobs: float32 [512, 64128], P('col', 'row')
Inputs may be any that keep to these rules, and one draw needn't show every extreme that they name: Among the 16 child beams of one index of row, at most 2 have their parents on the beams of any single index of row, and exactly 2 do for some index.
All inputs are finite; a program needn't handle non-finite values.
Results may differ from a plain program's by a relative error of at most 0.0015.
Values may be sent and summed in bfloat16 or wider, within the bound.
No kernel may reach another device: no remote copies, remote signals or barrier semaphores. Data moves between devices by JAX's collectives and lax.ppermute only.
A program may use at most 64 MiB of HBM per device.

v0:
```python
import jax
import jax.numpy as jnp
from jax import lax
from jax.sharding import PartitionSpec as P

HEAD_DIM = 128
D = 16384


def from_partner(value, axis, distance):
    mask = 2**distance
    pairs = [(source, source ^ mask) for source in range(lax.axis_size(axis))]
    return lax.ppermute(value, axis, pairs)


def count_before(sources):
    entries = sources.shape[-1]
    earlier = jnp.arange(entries)[:, None] > jnp.arange(entries)[None, :]
    matching = sources[..., :, None] == sources[..., None, :]
    return jnp.sum(matching & earlier, axis=-1)


def attend(queries_in, key_cache, value_cache, key_new, value_new, live_rows):
    leading = queries_in.shape[:-2]
    group_size = queries_in.shape[-2]
    panel_width = queries_in.shape[-1]
    head_part = min(panel_width, HEAD_DIM)
    heads_here = panel_width // head_part
    context = key_cache.shape[-2]
    query_heads = queries_in.reshape(leading + (group_size, heads_here, head_part))
    key_heads = key_cache.reshape(leading + (context, heads_here, head_part))
    value_heads = value_cache.reshape(leading + (context, heads_here, head_part))
    fresh_key = key_new.reshape(leading + (heads_here, head_part))
    fresh_value = value_new.reshape(leading + (1, heads_here, head_part)).astype(jnp.float32)
    cached = jnp.einsum(
        "...jhe,...the->...jht", query_heads, key_heads, preferred_element_type=jnp.float32
    )
    own_score = jnp.einsum(
        "...jhe,...he->...jh", query_heads, fresh_key, preferred_element_type=jnp.float32
    )
    other_cached, other_own = from_partner((cached, own_score), "col", 0)
    cached = cached + other_cached
    own_score = own_score + other_own
    scale_factor = HEAD_DIM ** (-0.5)
    cached = cached * scale_factor
    own_score = own_score * scale_factor
    positions = lax.broadcasted_iota(jnp.int32, cached.shape, cached.ndim - 1)
    visible = positions < live_rows.reshape(leading + (1, 1, 1))
    peak_score = jnp.maximum(jnp.max(jnp.where(visible, cached, -jnp.inf), axis=-1), own_score)
    weight = jnp.where(visible, jnp.exp(cached - peak_score[..., None]), jnp.float32(0.0))
    weight_own = jnp.exp(own_score - peak_score)
    weight_sum = jnp.sum(weight, axis=-1) + weight_own
    rounded = weight.astype(jnp.bfloat16)
    rounded_own = lax.optimization_barrier(weight_own.astype(jnp.bfloat16)).astype(jnp.float32)
    summed = jnp.einsum(
        "...jht,...the->...jhe", rounded, value_heads, preferred_element_type=jnp.float32
    )
    own_part = rounded_own[..., None] * fresh_value
    result = (summed + own_part) / weight_sum[..., None]
    return result.reshape(leading + (group_size, panel_width)).astype(jnp.bfloat16)


def body(
    queries,
    new_keys,
    new_values,
    cache_keys,
    cache_values,
    lengths,
    parents,
    residual,
    norm_gain,
    vocab_weight,
):
    row_count = lax.axis_size("row")
    beam_count = parents.shape[0]
    slot_cap = max(2, (2 * beam_count + row_count - 1) // row_count)
    my_row = lax.axis_index("row")
    group_size = queries.shape[1]
    panel_width = queries.shape[2]
    source = parents // beam_count
    rank_in = count_before(source)
    slot_index = source * slot_cap + rank_in
    slot_range = jnp.arange(slot_cap, dtype=jnp.int32)
    all_parents, all_lengths = (
        lax.all_gather(parents, "row", axis=0, tiled=True),
        lax.all_gather(lengths, "row", axis=0, tiled=True),
    )
    parent_table = all_parents.reshape(row_count, beam_count)
    sources_all = parent_table // beam_count
    offsets_all = parent_table % beam_count
    ranks_all = count_before(sources_all)
    chosen = (sources_all[:, None, :] == my_row) & (
        ranks_all[:, None, :] == slot_range[None, :, None]
    )
    rows_sent = jnp.sum(jnp.where(chosen, offsets_all[:, None, :], 0), axis=2)
    got_keys, got_values = (
        lax.all_to_all(cache_keys[rows_sent], "row", split_axis=0, concat_axis=0, tiled=True),
        lax.all_to_all(cache_values[rows_sent], "row", split_axis=0, concat_axis=0, tiled=True),
    )
    context = cache_keys.shape[1]
    kept_keys = got_keys.reshape(row_count * slot_cap, context, panel_width)[slot_index]
    kept_values = got_values.reshape(row_count * slot_cap, context, panel_width)[slot_index]
    attended = attend(queries, kept_keys, kept_values, new_keys, new_values, all_lengths[parents])
    stream = residual.astype(jnp.float32) + attended.astype(jnp.float32)
    square_sums = lax.psum(jnp.sum(stream * stream, axis=(1, 2)), "col")
    scaling = lax.rsqrt(square_sums / D + 1e-05)
    normed = (stream * norm_gain.astype(jnp.float32)[None] * scaling[:, None, None]).astype(
        jnp.bfloat16
    )
    gathered = lax.all_gather(normed, "row", axis=0, tiled=True)
    flat_rows = gathered.reshape(gathered.shape[0], group_size * panel_width)
    flat_weight = vocab_weight.reshape(group_size * panel_width, vocab_weight.shape[2])
    logits = lax.psum_scatter(
        jnp.dot(flat_rows, flat_weight, preferred_element_type=jnp.float32),
        "col",
        scatter_dimension=0,
        tiled=True,
    )
    totals = lax.psum(jnp.sum(jnp.exp(logits), axis=1), "row")
    return logits - jnp.log(totals)[:, None]


def solution(mesh):
    placed = (
        P("row", None, "col"),
        P("row", "col"),
        P("row", "col"),
        P("row", None, "col"),
        P("row", None, "col"),
        P("row"),
        P("row"),
        P("row", None, "col"),
        P(None, "col"),
        P(None, "col", "row"),
    )
    return jax.shard_map(
        body, mesh=mesh, in_specs=placed, out_specs=P("col", "row"), check_vma=False
    )
```

profile of v0, /device:TPU:1, one launch (start us, length us, event | category | flops | bytes accessed | tf_op | source)
XLA Modules:
  0.0 322.9 jit_solution(3743280184073839747)
XLA Ops:
  6.5 1.3 dynamic-slice
  8.5 0.9 dynamic-update-slice
  9.4 0.8 dynamic-update-slice.1
  10.2 14.4 %all-reduce.2 = (s32[512]{0:T(512)S(1)}, s32[512]{0:T(512)S(1)}) all-reduce(s32[512]{0:T(512)S(1)} %dynamic-update-slice, s32[512]{0:T(512)S(1)} %dynamic-update-slice.1), channel_id=1, replica_groups=mesh['row'=32,'col'=16] {'row'}, use_global_device_ids=true, to_apply=%add | all-reduce | flops 1024 | bytes 8192
  24.8 0.1 convert_reduce_fusion
  25.0 0.1 copy.27
  25.1 0.1 reshape.196
  25.2 1.7 gather_fusion.3
  26.9 11.0 %all-to-all-start.1 = ((bf16[32,2,128,64]{2,3,1,0:T(8,128)(2,1)}), bf16[32,2,128,64]{2,3,1,0:T(8,128)(2,1)S(1)}, u32[]{:S(2)}, u32[]{:S(2)}) async-start(bf16[32,2,128,64]{2,3,1,0:T(8,128)(2,1)} %bitcast.4), calls=%async_computation.1 | async-start | bytes 2097152 | tf_op jit(solution)/shard_map/all_to_all | solution.py:98
  37.9 1.7 gather_fusion
  39.6 15.3 %all-to-all-done.1 = bf16[32,2,128,64]{2,3,1,0:T(8,128)(2,1)S(1)} async-done(((bf16[32,2,128,64]{2,3,1,0:T(8,128)(2,1)}), bf16[32,2,128,64]{2,3,1,0:T(8,128)(2,1)S(1)}, u32[]{:S(2)}, u32[]{:S(2)}) %all-to-all-start.1) | async-done | bytes 1048608 | tf_op jit(solution)/shard_map/all_to_all | solution.py:98
  54.9 4.0 %all-to-all-start = ((bf16[32,2,128,64]{2,3,1,0:T(8,128)(2,1)}), bf16[32,2,128,64]{2,3,1,0:T(8,128)(2,1)S(1)}, u32[]{:S(2)}, u32[]{:S(2)}) async-start(bf16[32,2,128,64]{2,3,1,0:T(8,128)(2,1)} %bitcast.2), calls=%async_computation | async-start | bytes 2097152 | tf_op jit(solution)/shard_map/all_to_all | solution.py:99
  59.0 0.2 convert_reduce_fusion.1
  59.2 0.6 gather_fusion.4
  59.8 0.2 convolution_bitcast_fusion.1
  60.0 1.9 collective-permute-start
  61.9 0.1 fusion.16
  62.1 3.4 %collective-permute-start.1 = (f32[16,16,1]{1,0,2:T(8,128)S(1)}, f32[16,16,1]{1,0,2:T(8,128)S(1)}, u32[]{:S(2)}, u32[]{:S(2)}) collective-permute-start(f32[16,16,1]{1,0,2:T(8,128)S(1)} %bitcast.75), channel_id=1, source_target_pairs={{0,1},{1,0},{2,3},{3,2},{4,5},{5,4},{6,7},{7,6},{8,9},{9,8},{10,11... | collective-permute-start | bytes 3080 | tf_op jit(solution)/shard_map/ppermute | solution.py:13
  65.5 0.7 gather_fusion.2
  66.2 9.9 %all-to-all-done = bf16[32,2,128,64]{2,3,1,0:T(8,128)(2,1)S(1)} async-done(((bf16[32,2,128,64]{2,3,1,0:T(8,128)(2,1)}), bf16[32,2,128,64]{2,3,1,0:T(8,128)(2,1)S(1)}, u32[]{:S(2)}, u32[]{:S(2)}) %all-to-all-start) | async-done | bytes 1048608 | tf_op jit(solution)/shard_map/all_to_all | solution.py:99
  76.1 0.6 gather_fusion.1
  76.7 0.2 select_reduce_fusion
  76.9 0.2 fusion.7
  77.2 0.4 multiply_reduce_fusion
  77.6 26.0 %psum.14 = f32[16]{0:T(128)S(1)} all-reduce(f32[16]{0:T(128)S(1)} %get-tuple-element.13), channel_id=1, replica_groups=mesh['row'=32,'col'=16] {'col'}, use_global_device_ids=true, to_apply=%region_6.7 | all-reduce | flops 16 | bytes 128 | tf_op jit(solution)/shard_map/psum | solution.py:106
  103.6 0.7 multiply_convert_fusion
  104.4 58.6 %all-gather.2.cloned.1.call-done = bf16[512,16,64]{2,1,0:T(8,128)(2,1)} async-done(((bf16[16,16,64]{2,1,0:T(8,128)(2,1)}), bf16[512,16,64]{2,1,0:T(8,128)(2,1)}) %all-gather.2.cloned.1.call-update) | async-done | bytes 1048592 | tf_op jit(solution)/shard_map/all_gather | solution.py:111
  163.0 7.4 %convolution_bitcast_fusion = f32[512,2004]{1,0:T(8,128)} fusion(bf16[16,64,2004]{2,1,0:T(8,128)(2,1)} %param.19, bf16[512,16,64]{2,1,0:T(8,128)(2,1)} %all-gather.2.cloned.1.call-done), kind=kOutput, calls=%fused_computation.5 | convolution fusion | flops 2101346304 | bytes 9256960 | tf_op jit(solution)/shard_map/dot_general | solution.py:115
  170.5 69.5 %reduce-scatter.2.cloned.1.call-done = f32[32,2004]{1,0:T(8,128)} async-done(((f32[512,2004]{1,0:T(8,128)}), f32[32,2004]{1,0:T(8,128)}) %reduce-scatter.2.cloned.1.call-update) | async-done | bytes 256528 | tf_op jit(solution)/shard_map/reduce_scatter | solution.py:114
  240.0 1.1 exponential_reduce_fusion
  241.1 73.2 %psum.15 = f32[32]{0:T(128)S(1)} all-reduce(f32[32]{0:T(128)S(1)} %exponential_reduce_fusion), channel_id=1, replica_groups=mesh['row'=32,'col'=16] {'row'}, use_global_device_ids=true, to_apply=%region_9.10 | all-reduce | flops 32 | bytes 256 | tf_op jit(solution)/shard_map/psum | solution.py:120
  314.3 1.7 broadcast_subtract_fusion
  (43 shorter events, 0.5 us)
Async XLA Ops:
  6.5 18.7 %copy-start = (bf16[16,128,64]{1,2,0:T(8,128)(2,1)S(1)}, bf16[16,128,64]{1,2,0:T(8,128)(2,1)}, u32[]{:S(2)}) copy-start(bf16[16,128,64]{1,2,0:T(8,128)(2,1)} %param.13) | copy-start | bytes 786436
  26.9 11.0 %copy-start.1 = (bf16[16,128,64]{1,2,0:T(8,128)(2,1)S(1)}, bf16[16,128,64]{1,2,0:T(8,128)(2,1)}, u32[]{:S(2)}) copy-start(bf16[16,128,64]{1,2,0:T(8,128)(2,1)} %param.14) | copy-start | bytes 786436
  26.9 28.1 %all-to-all-start.1 = ((bf16[32,2,128,64]{2,3,1,0:T(8,128)(2,1)}), bf16[32,2,128,64]{2,3,1,0:T(8,128)(2,1)S(1)}, u32[]{:S(2)}, u32[]{:S(2)}) async-start(bf16[32,2,128,64]{2,3,1,0:T(8,128)(2,1)} %bitcast.4), calls=%async_computation.1 | async-start | bytes 2097152 | tf_op jit(solution)/shard_map/all_to_all | solution.py:98
  39.6 19.4 %copy-start.7 = (s32[16]{0:T(128)S(1)}, s32[16]{0:T(128)}, u32[]{:S(2)}) copy-start(s32[16]{0:T(128)} %param.16) | copy-start | bytes 196
  39.6 20.2 %copy-start.2 = (bf16[16,16,64]{2,1,0:T(8,128)(2,1)S(1)}, bf16[16,16,64]{2,1,0:T(8,128)(2,1)}, u32[]{:S(2)}) copy-start(bf16[16,16,64]{2,1,0:T(8,128)(2,1)} %param.10) | copy-start | bytes 98308
  39.6 22.3 %copy-start.6 = (bf16[16,64]{1,0:T(8,128)(2,1)S(1)}, bf16[16,64]{1,0:T(8,128)(2,1)}, u32[]{:S(2)}) copy-start(bf16[16,64]{1,0:T(8,128)(2,1)} %param.11) | copy-start | bytes 6148
  39.6 25.8 %copy-start.3 = (bf16[16,64]{1,0:T(8,128)(2,1)S(1)}, bf16[16,64]{1,0:T(8,128)(2,1)}, u32[]{:S(2)}) copy-start(bf16[16,64]{1,0:T(8,128)(2,1)} %param.12) | copy-start | bytes 6148
  39.6 25.9 %copy-start.4 = (bf16[16,64]{1,0:T(8,128)(2,1)S(1)}, bf16[16,64]{1,0:T(8,128)(2,1)}, u32[]{:S(2)}) copy-start(bf16[16,64]{1,0:T(8,128)(2,1)} %param.18) | copy-start | bytes 6148
  54.9 21.1 %all-to-all-start = ((bf16[32,2,128,64]{2,3,1,0:T(8,128)(2,1)}), bf16[32,2,128,64]{2,3,1,0:T(8,128)(2,1)S(1)}, u32[]{:S(2)}, u32[]{:S(2)}) async-start(bf16[32,2,128,64]{2,3,1,0:T(8,128)(2,1)} %bitcast.2), calls=%async_computation | async-start | bytes 2097152 | tf_op jit(solution)/shard_map/all_to_all | solution.py:99
  58.9 18.2 %copy-start.5 = (bf16[16,16,64]{2,1,0:T(8,128)(2,1)S(1)}, bf16[16,16,64]{2,1,0:T(8,128)(2,1)}, u32[]{:S(2)}) copy-start(bf16[16,16,64]{2,1,0:T(8,128)(2,1)} %param.17) | copy-start | bytes 98308
  58.9 104.1 %all-gather.2.cloned.1.call-start = ((), (), s32[]{:S(2)}) async-start(), calls=%async_computation.3 | async-start | bytes 2162688 | tf_op jit(solution)/shard_map/all_gather | solution.py:111
  60.0 16.7 %collective-permute-start = (f32[16,16,1,128]{3,1,0,2:T(8,128)S(1)}, f32[16,16,1,128]{3,1,0,2:T(8,128)S(1)}, u32[]{:S(2)}, u32[]{:S(2)}) collective-permute-start(f32[16,16,1,128]{3,1,0,2:T(8,128)S(1)} %convolution_bitcast_fusion.1), channel_id=1, source_target_pairs={{0,1},{1,0},{2,3},{3,2},{4,5},{5,4},{6,7},{7,6},{8,9},{9,8},{10,11... | collective-permute-start | bytes 393224 | tf_op jit(solution)/shard_map/ppermute | solution.py:13
  62.1 14.8 %collective-permute-start.1 = (f32[16,16,1]{1,0,2:T(8,128)S(1)}, f32[16,16,1]{1,0,2:T(8,128)S(1)}, u32[]{:S(2)}, u32[]{:S(2)}) collective-permute-start(f32[16,16,1]{1,0,2:T(8,128)S(1)} %bitcast.75), channel_id=1, source_target_pairs={{0,1},{1,0},{2,3},{3,2},{4,5},{5,4},{6,7},{7,6},{8,9},{9,8},{10,11... | collective-permute-start | bytes 3080 | tf_op jit(solution)/shard_map/ppermute | solution.py:13
  104.4 135.6 %reduce-scatter.2.cloned.1.call-start = ((), (), s32[]{:S(2)}) async-start(), calls=%async_computation.4 | async-start | bytes 4456448 | tf_op jit(solution)/shard_map/reduce_scatter | solution.py:114
Sparse Core Ops, SparseCore 0:
  104.5 58.4 all-gather.1
  170.6 69.3 reduce-scatter.1
where the time goes:
time: 323 us
  waiting for transfers between devices  153 us (47%)
  blocking collectives  114 us (35%)
  starting transfers between devices  20.3 us (6%)
  between operations  14.3 us (4%)
  local copies, waits for them, and re-layouts  8.63 us (3%)
  matrix products  8.17 us (3%)
  other arithmetic  4.38 us (1%)
    psum x1, blocking collectives, body(): totals = lax.psum(jnp.sum(jnp.exp(logits), axis=1), 'row')  73.2 us
    reduce_scatter x1, waiting for transfers between devices, body(): lax.psum_scatter(jnp.dot(flat_rows, flat_weight, preferred_element_type=j...  69.5 us
    all_gather x1, waiting for transfers between devices, body(): gathered = lax.all_gather(normed, 'row', axis=0, tiled=True)  58.6 us
    psum x1, blocking collectives, body(): square_sums = lax.psum(jnp.sum(stream * stream, axis=(1, 2)), 'col')  26 us
    all_to_all x1, waiting for transfers between devices, body(): lax.all_to_all(cache_keys[rows_sent], 'row', split_axis=0, concat_axis=0,...  15.3 us
    unnamed x1, blocking collectives  14.4 us
    all_to_all x1, starting transfers between devices, body(): lax.all_to_all(cache_keys[rows_sent], 'row', split_axis=0, concat_axis=0,...  11 us
    all_to_all x1, waiting for transfers between devices, body(): lax.all_to_all(cache_values[rows_sent], 'row', split_axis=0, concat_axis=...  9.9 us
  transfers between devices with their start and end apart: 6, of which 4 were waited for; matrix products, arithmetic and copies ran while one was open for 1% of the time, Pallas kernels for 0%

commit v1 on v0

--- a/solution.py
+++ b/solution.py
@@ -108,7 +108,9 @@
     normed = (stream * norm_gain.astype(jnp.float32)[None] * scaling[:, None, None]).astype(
         jnp.bfloat16
     )
-    gathered = lax.all_gather(normed, "row", axis=0, tiled=True)
+    gathered = jnp.concatenate(
+        lax.all_to_all(jnp.stack([normed] * lax.axis_size("row")), "row", 0, 0), axis=0
+    )
     flat_rows = gathered.reshape(gathered.shape[0], group_size * panel_width)
     flat_weight = vocab_weight.reshape(group_size * panel_width, vocab_weight.shape[2])
     logits = lax.psum_scatter(

time: 323 us -> 292 us (0.904)
  waiting for transfers between devices: 153 us -> 88 us
  blocking collectives: 114 us -> 142 us
  local copies, waits for them, and re-layouts: 8.63 us -> 15.8 us
    all_gather x1 -> x0, waiting for transfers between devices: 58.6 us -> none  [body(): gathered = lax.all_gather(normed, 'row', axis=0, tiled=True)]
    all_to_all x0 -> x1, blocking collectives: none -> 28.1 us  [body(): lax.all_to_all(jnp.stack([normed] * lax.axis_size('row')), 'row', 0, 0)]
    reduce_scatter x1, waiting for transfers between devices: 69.5 us -> 62.8 us  [body(): lax.psum_scatter(jnp.dot(flat_rows, flat_weight, preferred_element_type=j...]
    unnamed x21 -> x23, local copies, waits for them, and re-layouts: 3.04 us -> 8.29 us
  transfers between devices with their start and end apart: 6 -> 5, of which waited for: 4 -> 3; matrix products, arithmetic and copies ran while one was open for 1% -> 1% of each run, Pallas kernels for 0% -> 0%
where the time goes in v1:
time: 292 us; the launch traced here: 291 us
  blocking collectives  142 us (49%)
  waiting for transfers between devices  88 us (30%)
  starting transfers between devices  20.3 us (7%)
  local copies, waits for them, and re-layouts  15.8 us (5%)
  between operations  14.4 us (5%)
  matrix products  7.2 us (2%)
  other arithmetic  3.75 us (1%)
    psum x1, blocking collectives, body(): totals = lax.psum(jnp.sum(jnp.exp(logits), axis=1), 'row')  73.1 us
    reduce_scatter x1, waiting for transfers between devices, body(): lax.psum_scatter(jnp.dot(flat_rows, flat_weight, preferred_element_type=j...  62.8 us
    all_to_all x1, blocking collectives, body(): lax.all_to_all(jnp.stack([normed] * lax.axis_size('row')), 'row', 0, 0)  28.1 us
    psum x1, blocking collectives, body(): square_sums = lax.psum(jnp.sum(stream * stream, axis=(1, 2)), 'col')  26 us
    all_to_all x1, waiting for transfers between devices, body(): lax.all_to_all(cache_keys[rows_sent], 'row', split_axis=0, concat_axis=0,...  15.3 us
    unnamed x1, blocking collectives  14.4 us
    all_to_all x1, starting transfers between devices, body(): lax.all_to_all(cache_keys[rows_sent], 'row', split_axis=0, concat_axis=0,...  11 us
    all_to_all x1, waiting for transfers between devices, body(): lax.all_to_all(cache_values[rows_sent], 'row', split_axis=0, concat_axis=...  9.91 us
  transfers between devices with their start and end apart: 5, of which 3 were waited for; matrix products, arithmetic and copies ran while one was open for 1% of the time, Pallas kernels for 0%

profile of v1, /device:TPU:1, one launch (start us, length us, event | category | flops | bytes accessed | tf_op | source)
XLA Modules:
  0.0 291.1 jit_solution(15505381573584767959)
XLA Ops:
  6.6 1.3 dynamic-slice
  8.5 0.9 dynamic-update-slice
  9.4 0.8 dynamic-update-slice.1
  10.2 14.4 %all-reduce.2 = (s32[512]{0:T(512)S(1)}, s32[512]{0:T(512)S(1)}) all-reduce(s32[512]{0:T(512)S(1)} %dynamic-update-slice, s32[512]{0:T(512)S(1)} %dynamic-update-slice.1), channel_id=1, replica_groups=mesh['row'=32,'col'=16] {'row'}, use_global_device_ids=true, to_apply=%add | all-reduce | flops 1024 | bytes 8192
  25.2 1.7 gather_fusion.3
  26.9 11.0 %all-to-all-start.1 = ((bf16[32,2,128,64]{2,3,1,0:T(8,128)(2,1)}), bf16[32,2,128,64]{2,3,1,0:T(8,128)(2,1)S(1)}, u32[]{:S(2)}, u32[]{:S(2)}) async-start(bf16[32,2,128,64]{2,3,1,0:T(8,128)(2,1)} %bitcast.4), calls=%async_computation.1 | async-start | bytes 2097152 | tf_op jit(solution)/shard_map/all_to_all | solution.py:98
  38.0 1.7 gather_fusion
  39.7 15.3 %all-to-all-done.1 = bf16[32,2,128,64]{2,3,1,0:T(8,128)(2,1)S(1)} async-done(((bf16[32,2,128,64]{2,3,1,0:T(8,128)(2,1)}), bf16[32,2,128,64]{2,3,1,0:T(8,128)(2,1)S(1)}, u32[]{:S(2)}, u32[]{:S(2)}) %all-to-all-start.1) | async-done | bytes 1048608 | tf_op jit(solution)/shard_map/all_to_all | solution.py:98
  55.0 4.0 %all-to-all-start = ((bf16[32,2,128,64]{2,3,1,0:T(8,128)(2,1)}), bf16[32,2,128,64]{2,3,1,0:T(8,128)(2,1)S(1)}, u32[]{:S(2)}, u32[]{:S(2)}) async-start(bf16[32,2,128,64]{2,3,1,0:T(8,128)(2,1)} %bitcast.2), calls=%async_computation | async-start | bytes 2097152 | tf_op jit(solution)/shard_map/all_to_all | solution.py:99
  59.0 0.2 convert_reduce_fusion.1
  59.2 0.6 gather_fusion.4
  59.8 0.2 convolution_bitcast_fusion
  60.0 1.9 collective-permute-start
  62.0 0.1 fusion.15
  62.1 3.4 %collective-permute-start.1 = (f32[16,16,1]{1,0,2:T(8,128)S(1)}, f32[16,16,1]{1,0,2:T(8,128)S(1)}, u32[]{:S(2)}, u32[]{:S(2)}) collective-permute-start(f32[16,16,1]{1,0,2:T(8,128)S(1)} %bitcast.77), channel_id=1, source_target_pairs={{0,1},{1,0},{2,3},{3,2},{4,5},{5,4},{6,7},{7,6},{8,9},{9,8},{10,11... | collective-permute-start | bytes 3080 | tf_op jit(solution)/shard_map/ppermute | solution.py:13
  65.5 0.7 gather_fusion.2
  66.2 9.9 %all-to-all-done = bf16[32,2,128,64]{2,3,1,0:T(8,128)(2,1)S(1)} async-done(((bf16[32,2,128,64]{2,3,1,0:T(8,128)(2,1)}), bf16[32,2,128,64]{2,3,1,0:T(8,128)(2,1)S(1)}, u32[]{:S(2)}, u32[]{:S(2)}) %all-to-all-start) | async-done | bytes 1048608 | tf_op jit(solution)/shard_map/all_to_all | solution.py:99
  76.1 0.6 gather_fusion.1
  76.7 0.2 select_reduce_fusion
  76.9 0.2 fusion.6
  77.2 0.4 multiply_reduce_fusion
  77.6 26.0 %psum.14 = f32[16]{0:T(128)S(1)} all-reduce(f32[16]{0:T(128)S(1)} %get-tuple-element.13), channel_id=1, replica_groups=mesh['row'=32,'col'=16] {'col'}, use_global_device_ids=true, to_apply=%region_6.7 | all-reduce | flops 16 | bytes 128 | tf_op jit(solution)/shard_map/psum | solution.py:106
  103.8 0.5 stack.2
  104.2 1.5 reshape.255
  105.7 28.1 %all_to_all.15 = bf16[32,2,8192]{2,1,0:T(2,128)(2,1)} all-to-all(bf16[32,2,8192]{2,1,0:T(2,128)(2,1)S(1)} %reshape.255), channel_id=1, replica_groups=mesh['row'=32,'col'=16] {'row'}, dimensions={0} | all-to-all | bytes 2097152 | tf_op jit(solution)/shard_map/all_to_all | solution.py:112
  133.9 3.8 %reshape.256 = bf16[32,16,16,64]{3,2,1,0:T(8,128)(2,1)S(1)} reshape(bf16[32,2,8192]{2,1,0:T(2,128)(2,1)} %all_to_all.15) | data formatting | bytes 2097152
  137.6 1.5 reshape_reshape.3
  139.1 6.5 %fusion.22 = f32[512,2004]{1,0:T(8,128)} fusion(bf16[512,1024]{1,0:T(8,128)(2,1)S(1)} %reshape_reshape.3, bf16[1024,2004]{1,0:T(8,128)(2,1)} %bitcast.80), kind=kOutput, calls=%fused_computation.64 | convolution fusion | flops 2101346304 | bytes 9256960 | tf_op jit(solution)/shard_map/dot_general | solution.py:117
  145.6 62.8 %reduce-scatter.2.cloned.1.call-done = f32[32,2004]{1,0:T(8,128)} async-done(((f32[512,2004]{1,0:T(8,128)}), f32[32,2004]{1,0:T(8,128)}) %reduce-scatter.2.cloned.1.call-update) | async-done | bytes 256528 | tf_op jit(solution)/shard_map/reduce_scatter | solution.py:116
  208.4 1.1 exponential_reduce_fusion
  209.5 73.1 %psum.15 = f32[32]{0:T(128)S(1)} all-reduce(f32[32]{0:T(128)S(1)} %exponential_reduce_fusion), channel_id=1, replica_groups=mesh['row'=32,'col'=16] {'row'}, use_global_device_ids=true, to_apply=%region_9.10 | all-reduce | flops 32 | bytes 256 | tf_op jit(solution)/shard_map/psum | solution.py:122
  282.5 1.7 broadcast_subtract_fusion
  (45 shorter events, 0.8 us)
Async XLA Ops:
  6.5 18.7 %copy-start = (bf16[16,128,64]{1,2,0:T(8,128)(2,1)S(1)}, bf16[16,128,64]{1,2,0:T(8,128)(2,1)}, u32[]{:S(2)}) copy-start(bf16[16,128,64]{1,2,0:T(8,128)(2,1)} %param.13) | copy-start | bytes 786436
  6.5 31.4 %copy-start.1 = (bf16[16,128,64]{1,2,0:T(8,128)(2,1)S(1)}, bf16[16,128,64]{1,2,0:T(8,128)(2,1)}, u32[]{:S(2)}) copy-start(bf16[16,128,64]{1,2,0:T(8,128)(2,1)} %param.14) | copy-start | bytes 786436
  26.9 32.1 %copy-start.7 = (s32[16]{0:T(128)S(1)}, s32[16]{0:T(128)}, u32[]{:S(2)}) copy-start(s32[16]{0:T(128)} %param.16) | copy-start | bytes 196
  26.9 28.1 %all-to-all-start.1 = ((bf16[32,2,128,64]{2,3,1,0:T(8,128)(2,1)}), bf16[32,2,128,64]{2,3,1,0:T(8,128)(2,1)S(1)}, u32[]{:S(2)}, u32[]{:S(2)}) async-start(bf16[32,2,128,64]{2,3,1,0:T(8,128)(2,1)} %bitcast.4), calls=%async_computation.1 | async-start | bytes 2097152 | tf_op jit(solution)/shard_map/all_to_all | solution.py:98
  37.9 21.9 %copy-start.2 = (bf16[16,16,64]{2,1,0:T(8,128)(2,1)S(1)}, bf16[16,16,64]{2,1,0:T(8,128)(2,1)}, u32[]{:S(2)}) copy-start(bf16[16,16,64]{2,1,0:T(8,128)(2,1)} %param.10) | copy-start | bytes 98308
  37.9 24.0 %copy-start.6 = (bf16[16,64]{1,0:T(8,128)(2,1)S(1)}, bf16[16,64]{1,0:T(8,128)(2,1)}, u32[]{:S(2)}) copy-start(bf16[16,64]{1,0:T(8,128)(2,1)} %param.11) | copy-start | bytes 6148
  38.0 27.5 %copy-start.3 = (bf16[16,64]{1,0:T(8,128)(2,1)S(1)}, bf16[16,64]{1,0:T(8,128)(2,1)}, u32[]{:S(2)}) copy-start(bf16[16,64]{1,0:T(8,128)(2,1)} %param.12) | copy-start | bytes 6148
  38.0 27.5 %copy-start.4 = (bf16[16,64]{1,0:T(8,128)(2,1)S(1)}, bf16[16,64]{1,0:T(8,128)(2,1)}, u32[]{:S(2)}) copy-start(bf16[16,64]{1,0:T(8,128)(2,1)} %param.18) | copy-start | bytes 6148
  38.0 39.2 %copy-start.5 = (bf16[16,16,64]{2,1,0:T(8,128)(2,1)S(1)}, bf16[16,16,64]{2,1,0:T(8,128)(2,1)}, u32[]{:S(2)}) copy-start(bf16[16,16,64]{2,1,0:T(8,128)(2,1)} %param.17) | copy-start | bytes 98308
  55.0 21.1 %all-to-all-start = ((bf16[32,2,128,64]{2,3,1,0:T(8,128)(2,1)}), bf16[32,2,128,64]{2,3,1,0:T(8,128)(2,1)S(1)}, u32[]{:S(2)}, u32[]{:S(2)}) async-start(bf16[32,2,128,64]{2,3,1,0:T(8,128)(2,1)} %bitcast.2), calls=%async_computation | async-start | bytes 2097152 | tf_op jit(solution)/shard_map/all_to_all | solution.py:99
  59.0 149.4 %reduce-scatter.2.cloned.1.call-start = ((), (), s32[]{:S(2)}) async-start(), calls=%async_computation.4 | async-start | bytes 4456448 | tf_op jit(solution)/shard_map/reduce_scatter | solution.py:116
  60.0 16.7 %collective-permute-start = (f32[16,16,1,128]{3,1,0,2:T(8,128)S(1)}, f32[16,16,1,128]{3,1,0,2:T(8,128)S(1)}, u32[]{:S(2)}, u32[]{:S(2)}) collective-permute-start(f32[16,16,1,128]{3,1,0,2:T(8,128)S(1)} %convolution_bitcast_fusion), channel_id=1, source_target_pairs={{0,1},{1,0},{2,3},{3,2},{4,5},{5,4},{6,7},{7,6},{8,9},{9,8},{10,11... | collective-permute-start | bytes 393224 | tf_op jit(solution)/shard_map/ppermute | solution.py:13
  62.1 14.8 %collective-permute-start.1 = (f32[16,16,1]{1,0,2:T(8,128)S(1)}, f32[16,16,1]{1,0,2:T(8,128)S(1)}, u32[]{:S(2)}, u32[]{:S(2)}) collective-permute-start(f32[16,16,1]{1,0,2:T(8,128)S(1)} %bitcast.77), channel_id=1, source_target_pairs={{0,1},{1,0},{2,3},{3,2},{4,5},{5,4},{6,7},{7,6},{8,9},{9,8},{10,11... | collective-permute-start | bytes 3080 | tf_op jit(solution)/shard_map/ppermute | solution.py:13
Sparse Core Ops, SparseCore 0:
  145.7 62.5 reduce-scatter.1
